TPU v7x, 32 devices: a whole 2x2x4 slice. The times are simulated.
32 devices in a mesh: surf: 8 (over z, y), vol: 4 (over x, core).
Axes of the slice: x: 2, y: 2, z: 4, core: 2. Of those that a mesh axis runs over, the one named last changes fastest.
Arguments:
- casting: bfloat16 [32768, 128], P(('surf', 'vol')), may hold values from -5 to 5, as said below
- owner: int32 [32768, 1], P(('surf', 'vol')), may hold values from 0 to 31; in each aligned block of 1024 rows (0 to 1023, 1024 to 2047, ...) at most 128 rows name the same one
- face_id: int32 [32768], P(('surf', 'vol')), may hold values from 0 to 2047
- mold_faces: bfloat16 [65536, 128], P(('surf', 'vol')), may hold values from -5 to 5, as said below
- mortar_d: bfloat16 [64, 64], replicated, may hold values from -0.75 to 0.75
- mortar_m: bfloat16 [64, 64], replicated, may hold values from -0.75 to 0.75
- conduct: bfloat16 [128, 128], replicated, may hold values from -0.5 to 0.5
- volume: bfloat16 [65536, 128], P(('surf', 'vol')), may hold values from -6 to 6
Outputs:
- casting_out: bfloat16 [32768, 128], P(('surf', 'vol'))
- mold_out: bfloat16 [65536, 128], P(('surf', 'vol'))
Inputs may be any that keep to these rules, and one draw needn't show every extreme that they name: Among the 1024 rows of one device no owner is named more than 128 times, a bound that some block reaches. `casting`: temperatures lie within -5 to 5; conductances lie within 0.3 to 3. `mold_faces`: temperatures lie within -5 to 5; area weights lie within 0.3 to 3.
All inputs are finite; a program needn't handle non-finite values.
Results may differ from a plain program's by a relative error of at most 0.0055.
Values may be sent and summed in bfloat16 or wider, within the bound.
No kernel may reach another device: no remote copies, remote signals or barrier semaphores. Data moves between devices by JAX's collectives and lax.ppermute only.
A program may use at most 64 MiB of HBM per device.

v0:
```python
import math
import jax
import jax.numpy as jnp
from jax import lax
from jax.sharding import PartitionSpec as P

relax = 0.5


def contact(rows, mold_rows, stacked, joined, node_count):
    pair_rows = jnp.concatenate([rows[:, :node_count], mold_rows[:, :node_count]], axis=1)
    gap_jump = jnp.dot(pair_rows, stacked, preferred_element_type=jnp.float32)
    heat_flux = (
        rows[:, node_count:].astype(jnp.float32)
        * mold_rows[:, node_count:].astype(jnp.float32)
        * gap_jump
    ).astype(jnp.bfloat16)
    projected = jnp.dot(heat_flux, joined, preferred_element_type=jnp.float32)
    answer = jnp.concatenate([projected[:, :node_count], gap_jump], axis=1).astype(jnp.bfloat16)
    gained = projected[:, node_count:].astype(jnp.bfloat16)
    return (answer, gained)


def local(casting, owner, face_id, mold_faces, mortar_d, mortar_m, conduct, volume):
    seg_rows, row_width = casting.shape
    node_count = mortar_d.shape[0]
    face_rows = mold_faces.shape[0]
    surf_count = lax.axis_size("surf")
    vol_count = lax.axis_size("vol")
    devices = surf_count * vol_count
    capacity = 4 * seg_rows // devices
    slots = devices * capacity
    target = owner[:, 0]
    hits = (target[:, None] == jnp.arange(devices, dtype=jnp.int32)[None, :]).astype(jnp.int32)
    position = jnp.sum((jnp.cumsum(hits, axis=0) - 1) * hits, axis=1)
    slot_index = target * capacity + position
    send_ids = jnp.full((slots,), -1, jnp.int32).at[slot_index].set(face_id)
    block_rows = math.gcd(512, slots)
    turns = slots // block_rows
    stacked = jnp.concatenate([mortar_d.T, -mortar_m.T], axis=0)
    joined = jnp.concatenate([mortar_d, mortar_m], axis=1)
    face_range = jnp.arange(face_rows, dtype=jnp.int32)
    send_rows = jnp.zeros((slots, row_width), jnp.bfloat16).at[slot_index].set(casting)
    got_rows, got_ids = (
        lax.all_to_all(
            send_rows.reshape(devices, capacity, row_width),
            ("surf", "vol"),
            split_axis=0,
            concat_axis=0,
            tiled=True,
        ),
        lax.all_to_all(
            send_ids.reshape(devices, capacity),
            ("surf", "vol"),
            split_axis=0,
            concat_axis=0,
            tiled=True,
        ),
    )
    flat_rows = got_rows.reshape(turns, block_rows, row_width)
    flat_ids = got_ids.reshape(turns, block_rows)

    def settle(totals, pieces):
        rows, row_ids = pieces
        selector = (row_ids[:, None] == face_range[None, :]).astype(jnp.bfloat16)
        mold_rows = jnp.dot(selector, mold_faces, preferred_element_type=jnp.float32).astype(
            jnp.bfloat16
        )
        answer, gained = contact(rows, mold_rows, stacked, joined, node_count)
        totals = totals + lax.dot_general(
            selector, gained, (((0,), (0,)), ((), ())), preferred_element_type=jnp.float32
        )
        return (totals, answer)

    totals, answers = lax.scan(
        settle, jnp.zeros((face_rows, node_count), jnp.float32), (flat_rows, flat_ids)
    )
    returned = lax.all_to_all(
        answers.reshape(devices, capacity, row_width),
        ("surf", "vol"),
        split_axis=0,
        concat_axis=0,
        tiled=True,
    )
    casting_out = returned.reshape(slots, row_width)[slot_index]
    face_totals = totals.astype(jnp.bfloat16)
    quarter = face_rows // vol_count
    relaid = lax.all_to_all(
        face_totals.reshape(vol_count, quarter * node_count // row_width, row_width),
        "vol",
        split_axis=0,
        concat_axis=0,
        tiled=True,
    )
    heat = jnp.dot(volume, conduct, preferred_element_type=jnp.float32)
    placed = relaid.reshape(face_rows, node_count).astype(jnp.float32)
    inject = jnp.concatenate([placed, jnp.zeros((face_rows, node_count), jnp.float32)], axis=1)
    mold_out = (volume.astype(jnp.float32) + relax * (inject - heat)).astype(jnp.bfloat16)
    return (casting_out, mold_out)


def solution(mesh):
    return jax.shard_map(
        local,
        mesh=mesh,
        in_specs=(
            P(("surf", "vol"), None),
            P(("surf", "vol"), None),
            P(("surf", "vol")),
            P(("surf", "vol"), None),
            P(),
            P(),
            P(),
            P(("surf", "vol"), None),
        ),
        out_specs=(P(("surf", "vol"), None), P(("surf", "vol"), None)),
        check_vma=False,
    )
```

profile of v0, /device:TPU:0, one launch (start us, length us, event | category | flops | bytes accessed | tf_op | source)
XLA Modules:
  0.0 131.0 jit_solution(7700214398383684304)
XLA Ops:
  1.4 9.0 %reduce-window.6 = s32[32,8,128]{2,1,0:T(8,128)S(1)} reduce-window(s32[32,8,128]{2,1,0:T(8,128)S(1)} %fusion.23, s32[]{:T(128)} %constant.13.clone.1), window={size=1x1x128 pad=0_0x0_0x127_0}, to_apply=%region_0.0 | reduce-window | flops 4161536 | bytes 262148 | tf_op jit(solution)/shard_map/reduce-window
  11.0 5.1 %scatter_custom_fusion = s32[4096]{0:T(1024)} fusion(s32[1024]{0:T(1024)S(1)} %bitcast.65, s32[1024]{0:T(1024)} %param.12, s32[]{:T(128)} %constant.20.clone.1), kind=kCustom, calls=%fused_computation.44 | custom fusion | bytes 16896 | tf_op jit(solution)/shard_map/scatter | solution.py:37
  16.0 7.3 %all-to-all-start = ((s32[32,1,128]{2,1,0:T(1,128)}), s32[32,1,128]{2,1,0:T(1,128)S(1)}, u32[]{:S(2)}, u32[]{:S(2)}) async-start(s32[32,1,128]{2,1,0:T(1,128)} %bitcast.6), calls=%async_computation | async-start | bytes 32768 | tf_op jit(solution)/shard_map/all_to_all | solution.py:52
  23.3 4.7 %scatter_custom_fusion.1 = bf16[4096,128]{1,0:T(8,128)(2,1)} fusion(s32[1024]{0:T(1024)S(1)} %bitcast.66, bf16[1024,128]{1,0:T(8,128)(2,1)} %param.10, bf16[]{:T(256)} %constant.15.clone.1), kind=kCustom, calls=%fused_computation.31 | custom fusion | bytes 1049088 | tf_op jit(solution)/shard_map/scatter | solution.py:43
  28.0 2.4 %all-to-all-done = s32[32,1,128]{2,1,0:T(1,128)S(1)} async-done(((s32[32,1,128]{2,1,0:T(1,128)}), s32[32,1,128]{2,1,0:T(1,128)S(1)}, u32[]{:S(2)}, u32[]{:S(2)}) %all-to-all-start) | async-done | bytes 16416 | tf_op jit(solution)/shard_map/all_to_all | solution.py:52
  30.5 3.4 %all-to-all-start.1 = ((bf16[32,128,128]{2,1,0:T(8,128)(2,1)}), bf16[32,128,128]{2,1,0:T(8,128)(2,1)S(1)}, u32[]{:S(2)}, u32[]{:S(2)}) async-start(bf16[32,128,128]{2,1,0:T(8,128)(2,1)} %bitcast.7), calls=%async_computation.1 | async-start | bytes 2097152 | tf_op jit(solution)/shard_map/all_to_all | solution.py:45
  35.5 24.6 %all-to-all-done.1 = bf16[32,128,128]{2,1,0:T(8,128)(2,1)S(1)} async-done(((bf16[32,128,128]{2,1,0:T(8,128)(2,1)}), bf16[32,128,128]{2,1,0:T(8,128)(2,1)S(1)}, u32[]{:S(2)}, u32[]{:S(2)}) %all-to-all-start.1) | async-done | bytes 1048608 | tf_op jit(solution)/shard_map/all_to_all | solution.py:45
  60.1 28.5 %while.13 = (s32[]{:T(128)}, f32[2048,64]{0,1:T(8,128)S(1)}, bf16[8,512,128]{2,1,0:T(8,128)(2,1)}, s32[8,512]{1,0:T(8,128)S(1)}, bf16[8,512,128]{2,1,0:T(8,128)(...) while((s32[]{:T(128)}, f32[2048,64]{0,1:T(8,128)S(1)}, ...), condition=%wide.region_6.7_spmd.clone, body=%wide.region_5.6_spmd.clone.sunk | while | flops 422641664 | bytes 4366467 | solution.py:75
  60.1 1.1 fusion.44
  63.7 1.1 fusion.44
  67.2 1.1 fusion.44
  70.8 1.1 fusion.44
  72.7 1.0 fusion.46
  74.4 1.1 fusion.44
  77.9 1.1 fusion.44
  79.8 1.0 fusion.46
  81.5 1.1 fusion.44
  85.1 1.1 fusion.44
  86.9 1.0 fusion.46
  89.2 8.5 %all_to_all.24 = bf16[4,256,128]{2,1,0:T(8,128)(2,1)S(1)} all-to-all(bf16[4,256,128]{2,1,0:T(8,128)(2,1)S(1)} %reshape.89), channel_id=1, replica_groups=mesh['surf'=8,'vol'=4] {'vol'}, dimensions={0} | all-to-all | bytes 524288 | tf_op jit(solution)/shard_map/all_to_all | solution.py:88
  97.8 2.8 %all-to-all-start.2 = ((bf16[32,128,128]{2,1,0:T(8,128)(2,1)}), bf16[32,128,128]{2,1,0:T(8,128)(2,1)S(1)}, u32[]{:S(2)}, u32[]{:S(2)}) async-start(bf16[32,128,128]{2,1,0:T(8,128)(2,1)} %bitcast.11), calls=%async_computation.2 | async-start | bytes 2097152 | tf_op jit(solution)/shard_map/all_to_all | solution.py:78
  100.8 1.1 fusion.18
  102.0 24.8 %all-to-all-done.2 = bf16[32,128,128]{2,1,0:T(8,128)(2,1)S(1)} async-done(((bf16[32,128,128]{2,1,0:T(8,128)(2,1)}), bf16[32,128,128]{2,1,0:T(8,128)(2,1)S(1)}, u32[]{:S(2)}, u32[]{:S(2)}) %all-to-all-start.2) | async-done | bytes 1048608 | tf_op jit(solution)/shard_map/all_to_all | solution.py:78
  126.7 4.3 %gather_fusion = bf16[1024,128]{1,0:T(8,128)(2,1)} fusion(bf16[4096,128]{1,0:T(8,128)(2,1)S(1)} %bitcast.55, s32[1024]{0:T(1024)S(1)} %broadcast_clamp_fusion), kind=kCustom, calls=%fused_computation | custom fusion | bytes 528384 | tf_op jit(solution)/shard_map/gather | solution.py:85
  (137 shorter events, 19.8 us)
Async XLA Ops:
  0.6 100.2 %copy-start = (bf16[128,128]{1,0:T(8,128)(2,1)S(1)}, bf16[128,128]{1,0:T(8,128)(2,1)}, u32[]{:S(2)}) copy-start(bf16[128,128]{1,0:T(8,128)(2,1)} %param.16) | copy-start | bytes 98308
  0.6 10.2 %copy-start.4 = (s32[1024,1]{0,1:T(1,128)S(1)}, s32[1024,1]{0,1:T(1,128)}, u32[]{:S(2)}) copy-start(s32[1024,1]{0,1:T(1,128)} %param.11) | copy-start | bytes 12292
  16.0 14.4 %all-to-all-start = ((s32[32,1,128]{2,1,0:T(1,128)}), s32[32,1,128]{2,1,0:T(1,128)S(1)}, u32[]{:S(2)}, u32[]{:S(2)}) async-start(s32[32,1,128]{2,1,0:T(1,128)} %bitcast.6), calls=%async_computation | async-start | bytes 32768 | tf_op jit(solution)/shard_map/all_to_all | solution.py:52
  30.5 3.5 %copy-start.3 = (bf16[64,64]{1,0:T(8,128)(2,1)S(1)}, bf16[64,64]{1,0:T(8,128)(2,1)}, u32[]{:S(2)}) copy-start(bf16[64,64]{1,0:T(8,128)(2,1)} %param.14) | copy-start | bytes 24580
  30.5 3.6 %copy-start.2 = (bf16[64,64]{1,0:T(8,128)(2,1)S(1)}, bf16[64,64]{1,0:T(8,128)(2,1)}, u32[]{:S(2)}) copy-start(bf16[64,64]{1,0:T(8,128)(2,1)} %param.15) | copy-start | bytes 24580
  30.5 29.6 %copy-start.5 = (bf16[2048,128]{1,0:T(8,128)(2,1)S(1)}, bf16[2048,128]{1,0:T(8,128)(2,1)}, u32[]{:S(2)}) copy-start(bf16[2048,128]{1,0:T(8,128)(2,1)} %param.13) | copy-start | bytes 1572868
  30.5 29.6 %all-to-all-start.1 = ((bf16[32,128,128]{2,1,0:T(8,128)(2,1)}), bf16[32,128,128]{2,1,0:T(8,128)(2,1)S(1)}, u32[]{:S(2)}, u32[]{:S(2)}) async-start(bf16[32,128,128]{2,1,0:T(8,128)(2,1)} %bitcast.7), calls=%async_computation.1 | async-start | bytes 2097152 | tf_op jit(solution)/shard_map/all_to_all | solution.py:45
  97.8 3.1 %copy-start.1 = (bf16[2048,128]{1,0:T(8,128)(2,1)S(1)}, bf16[2048,128]{1,0:T(8,128)(2,1)}, u32[]{:S(2)}) copy-start(bf16[2048,128]{1,0:T(8,128)(2,1)} %param.17) | copy-start | bytes 1572868
  97.8 29.0 %all-to-all-start.2 = ((bf16[32,128,128]{2,1,0:T(8,128)(2,1)}), bf16[32,128,128]{2,1,0:T(8,128)(2,1)S(1)}, u32[]{:S(2)}, u32[]{:S(2)}) async-start(bf16[32,128,128]{2,1,0:T(8,128)(2,1)} %bitcast.11), calls=%async_computation.2 | async-start | bytes 2097152 | tf_op jit(solution)/shard_map/all_to_all | solution.py:78
where the time goes:
time: 131 us
  waiting for transfers between devices  51.8 us (40%)
  local copies, waits for them, and re-layouts  23.3 us (18%)
  matrix products  21.3 us (16%)
  starting transfers between devices  13.5 us (10%)
  other arithmetic  11 us (8%)
  blocking collectives  8.54 us (7%)
    all_to_all x1, waiting for transfers between devices, local(): lax.all_to_all(answers.reshape(devices, capacity, row_width), ('surf', 'v...  24.8 us
    all_to_all x1, waiting for transfers between devices, local(): lax.all_to_all(send_rows.reshape(devices, capacity, row_width), ('surf',...  24.6 us
    another operation x2, other arithmetic  9.04 us
    dot_general x8, matrix products, settle(): jnp.dot(selector, mold_faces, preferred_element_type=jnp.float32)  8.6 us
    all_to_all x1, blocking collectives, local(): lax.all_to_all(face_totals.reshape(vol_count, quarter * node_count // row...  8.54 us
    dot_general x8, matrix products, settle(): lax.dot_general(selector, gained, (((0,), (0,)), ((), ())), preferred_ele...  8.09 us
    all_to_all x1, starting transfers between devices, local(): lax.all_to_all(send_ids.reshape(devices, capacity), ('surf', 'vol'), spli...  7.33 us
    dynamic_update_slice x16, local copies, waits for them, and re-layouts, local(): lax.scan(settle, jnp.zeros((face_rows, node_count), jnp.float32), (flat_r...  6.25 us
  transfers between devices with their start and end apart: 3, of which 3 were waited for; matrix products, arithmetic and copies ran while one was open for 6% of the time, Pallas kernels for 0%

commit v1 on v0

--- a/solution.py
+++ b/solution.py
@@ -5,6 +5,17 @@
 from jax.sharding import PartitionSpec as P
 
 relax = 0.5
+
+
+def cut_along(shard, dim, size):
+    before, after = (shard.shape[:dim], shard.shape[dim + 1 :])
+    return jnp.moveaxis(shard.reshape(*before, size, -1, *after), dim, 0)
+
+
+def joined_along(pieces, dim):
+    shape = list(pieces.shape[1:])
+    shape[dim] *= pieces.shape[0]
+    return jnp.moveaxis(pieces, 0, dim).reshape(shape)
 
 
 def contact(rows, mold_rows, stacked, joined, node_count):
@@ -85,13 +96,15 @@
     casting_out = returned.reshape(slots, row_width)[slot_index]
     face_totals = totals.astype(jnp.bfloat16)
     quarter = face_rows // vol_count
-    relaid = lax.all_to_all(
-        face_totals.reshape(vol_count, quarter * node_count // row_width, row_width),
-        "vol",
-        split_axis=0,
-        concat_axis=0,
-        tiled=True,
-    )
+    value = face_totals.reshape(vol_count, quarter * node_count // row_width, row_width)
+    size, here = (lax.axis_size("vol"), lax.axis_index("vol"))
+    blocks = cut_along(value, 0, size)
+    outs = [blocks[here]]
+    for step in range(1, size):
+        sent = blocks[here ^ step]
+        outs.append(lax.ppermute(sent, "vol", [(i, i ^ step) for i in range(size)]))
+    blocks = jnp.stack(outs)[here ^ jnp.arange(size)]
+    relaid = joined_along(blocks, 0)
     heat = jnp.dot(volume, conduct, preferred_element_type=jnp.float32)
     placed = relaid.reshape(face_rows, node_count).astype(jnp.float32)
     inject = jnp.concatenate([placed, jnp.zeros((face_rows, node_count), jnp.float32)], axis=1)

time: 131 us -> 123 us (0.939)
  blocking collectives: 8.54 us -> 0 us
  waiting for transfers between devices: 51.8 us -> 48.6 us
  starting transfers between devices: 13.5 us -> 16.3 us
    all_to_all x1, waiting for transfers between devices: 24.8 us -> 10.6 us  [local(): lax.all_to_all(answers.reshape(devices, capacity, row_width), ('surf', 'v...]
    ppermute x0 -> x3, waiting for transfers between devices: none -> 10.9 us  [local(): outs.append(lax.ppermute(sent, 'vol', [(i, i ^ step) for i in range(size)]))]
    all_to_all x1 -> x0, blocking collectives: 8.54 us -> none  [local(): lax.all_to_all(face_totals.reshape(vol_count, quarter * node_count // row...]
    ppermute x0 -> x3, starting transfers between devices: none -> 1.95 us  [local(): outs.append(lax.ppermute(sent, 'vol', [(i, i ^ step) for i in range(size)]))]
    another operation x2 -> x3, other arithmetic: 9.04 us -> 9.08 us
  transfers between devices with their start and end apart: 3 -> 6, of which waited for: 3 -> 5; matrix products, arithmetic and copies ran while one was open for 6% -> 7% of each run, Pallas kernels for 0% -> 0%
where the time goes in v1:
time: 123 us
  waiting for transfers between devices  48.6 us (40%)
  local copies, waits for them, and re-layouts  23.9 us (19%)
  matrix products  21.2 us (17%)
  starting transfers between devices  16.3 us (13%)
  other arithmetic  11 us (9%)
    all_to_all x1, waiting for transfers between devices, local(): lax.all_to_all(send_rows.reshape(devices, capacity, row_width), ('surf',...  24.6 us
    ppermute x3, waiting for transfers between devices, local(): outs.append(lax.ppermute(sent, 'vol', [(i, i ^ step) for i in range(size)]))  10.9 us
    all_to_all x1, waiting for transfers between devices, local(): lax.all_to_all(answers.reshape(devices, capacity, row_width), ('surf', 'v...  10.6 us
    another operation x2, other arithmetic  9.04 us
    dot_general x8, matrix products, settle(): jnp.dot(selector, mold_faces, preferred_element_type=jnp.float32)  8.58 us
    dot_general x8, matrix products, settle(): lax.dot_general(selector, gained, (((0,), (0,)), ((), ())), preferred_ele...  8.07 us
    all_to_all x1, starting transfers between devices, local(): lax.all_to_all(send_ids.reshape(devices, capacity), ('surf', 'vol'), spli...  7.33 us
    dynamic_update_slice x16, local copies, waits for them, and re-layouts, local(): lax.scan(settle, jnp.zeros((face_rows, node_count), jnp.float32), (flat_r...  6.24 us
  transfers between devices with their start and end apart: 6, of which 5 were waited for; matrix products, arithmetic and copies ran while one was open for 7% of the time, Pallas kernels for 0%

profile of v1, /device:TPU:0, one launch (start us, length us, event | category | flops | bytes accessed | tf_op | source)
XLA Modules:
  0.0 122.7 jit_solution(9898804971416143376)
XLA Ops:
  1.4 9.0 %reduce-window.6 = s32[32,8,128]{2,1,0:T(8,128)S(1)} reduce-window(s32[32,8,128]{2,1,0:T(8,128)S(1)} %fusion.23, s32[]{:T(128)} %constant.18.clone.1), window={size=1x1x128 pad=0_0x0_0x127_0}, to_apply=%region_0.0 | reduce-window | flops 4161536 | bytes 262148 | tf_op jit(solution)/shard_map/reduce-window
  11.0 5.1 %scatter_custom_fusion = s32[4096]{0:T(1024)} fusion(s32[1024]{0:T(1024)S(1)} %bitcast.79, s32[1024]{0:T(1024)} %param.12, s32[]{:T(128)} %constant.13.clone.1), kind=kCustom, calls=%fused_computation.49 | custom fusion | bytes 16896 | tf_op jit(solution)/shard_map/scatter | solution.py:48
  16.0 7.3 %all-to-all-start = ((s32[32,1,128]{2,1,0:T(1,128)}), s32[32,1,128]{2,1,0:T(1,128)S(1)}, u32[]{:S(2)}, u32[]{:S(2)}) async-start(s32[32,1,128]{2,1,0:T(1,128)} %bitcast.6), calls=%async_computation | async-start | bytes 32768 | tf_op jit(solution)/shard_map/all_to_all | solution.py:63
  23.3 4.7 %scatter_custom_fusion.1 = bf16[4096,128]{1,0:T(8,128)(2,1)} fusion(s32[1024]{0:T(1024)S(1)} %bitcast.80, bf16[1024,128]{1,0:T(8,128)(2,1)} %param.10, bf16[]{:T(256)} %constant.20.clone.1), kind=kCustom, calls=%fused_computation.32 | custom fusion | bytes 1049088 | tf_op jit(solution)/shard_map/scatter | solution.py:54
  28.0 2.4 %all-to-all-done = s32[32,1,128]{2,1,0:T(1,128)S(1)} async-done(((s32[32,1,128]{2,1,0:T(1,128)}), s32[32,1,128]{2,1,0:T(1,128)S(1)}, u32[]{:S(2)}, u32[]{:S(2)}) %all-to-all-start) | async-done | bytes 16416 | tf_op jit(solution)/shard_map/all_to_all | solution.py:63
  30.5 3.4 %all-to-all-start.1 = ((bf16[32,128,128]{2,1,0:T(8,128)(2,1)}), bf16[32,128,128]{2,1,0:T(8,128)(2,1)S(1)}, u32[]{:S(2)}, u32[]{:S(2)}) async-start(bf16[32,128,128]{2,1,0:T(8,128)(2,1)} %bitcast.7), calls=%async_computation.1 | async-start | bytes 2097152 | tf_op jit(solution)/shard_map/all_to_all | solution.py:56
  35.5 24.6 %all-to-all-done.1 = bf16[32,128,128]{2,1,0:T(8,128)(2,1)S(1)} async-done(((bf16[32,128,128]{2,1,0:T(8,128)(2,1)}), bf16[32,128,128]{2,1,0:T(8,128)(2,1)S(1)}, u32[]{:S(2)}, u32[]{:S(2)}) %all-to-all-start.1) | async-done | bytes 1048608 | tf_op jit(solution)/shard_map/all_to_all | solution.py:56
  60.1 28.5 %while.13 = (s32[]{:T(128)}, f32[2048,64]{0,1:T(8,128)S(1)}, bf16[8,512,128]{2,1,0:T(8,128)(2,1)}, s32[8,512]{1,0:T(8,128)S(1)}, bf16[8,512,128]{2,1,0:T(8,128)(...) while((s32[]{:T(128)}, f32[2048,64]{0,1:T(8,128)S(1)}, ...), condition=%wide.region_6.7_spmd.clone, body=%wide.region_5.6_spmd.clone.sunk | while | flops 422641664 | bytes 4366467 | solution.py:86
  60.1 1.1 fusion.45
  61.8 1.0 fusion.47
  63.7 1.1 fusion.45
  67.2 1.1 fusion.45
  70.8 1.1 fusion.45
  74.3 1.1 fusion.45
  77.9 1.1 fusion.45
  81.4 1.1 fusion.45
  85.0 1.1 fusion.45
  88.6 3.6 %all-to-all-start.2 = ((bf16[32,128,128]{2,1,0:T(8,128)(2,1)}), bf16[32,128,128]{2,1,0:T(8,128)(2,1)S(1)}, u32[]{:S(2)}, u32[]{:S(2)}) async-start(bf16[32,128,128]{2,1,0:T(8,128)(2,1)} %bitcast.11), calls=%async_computation.2 | async-start | bytes 2097152 | tf_op jit(solution)/shard_map/all_to_all | solution.py:89
  92.9 1.6 %collective-permute-start.2 = (bf16[1,256,128]{2,1,0:T(8,128)(2,1)S(1)}, bf16[1,256,128]{2,1,0:T(8,128)(2,1)S(1)}, u32[]{:S(2)}, u32[]{:S(2)}) collective-permute-start(bf16[1,256,128]{2,1,0:T(8,128)(2,1)S(1)} %get-tuple-element.114), channel_id=1, source_target_pairs={{0,3},{1,2},{2,1},{3,0},{4,7},{5,6},{6,5},{7,4},{8,11},{9,10},{10,... | collective-permute-start | bytes 196616 | tf_op jit(solution)/shard_map/ppermute | solution.py:105
  94.8 7.0 %collective-permute-done.2 = bf16[1,256,128]{2,1,0:T(8,128)(2,1)S(1)} collective-permute-done((bf16[1,256,128]{2,1,0:T(8,128)(2,1)S(1)}, bf16[1,256,128]{2,1,0:T(8,128)(2,1)S(1)}, u32[]{:S(2)}, u32[]{:S(2)}) %collective-permute-start.2) | collective-permute-done | bytes 65568 | tf_op jit(solution)/shard_map/ppermute | solution.py:105
  101.9 3.8 %collective-permute-done.1 = bf16[1,256,128]{2,1,0:T(8,128)(2,1)S(1)} collective-permute-done((bf16[1,256,128]{2,1,0:T(8,128)(2,1)S(1)}, bf16[1,256,128]{2,1,0:T(8,128)(2,1)S(1)}, u32[]{:S(2)}, u32[]{:S(2)}) %collective-permute-start.1) | collective-permute-done | bytes 65568 | tf_op jit(solution)/shard_map/ppermute | solution.py:105
  106.6 1.1 fusion.18
  107.7 10.6 %all-to-all-done.2 = bf16[32,128,128]{2,1,0:T(8,128)(2,1)S(1)} async-done(((bf16[32,128,128]{2,1,0:T(8,128)(2,1)}), bf16[32,128,128]{2,1,0:T(8,128)(2,1)S(1)}, u32[]{:S(2)}, u32[]{:S(2)}) %all-to-all-start.2) | async-done | bytes 1048608 | tf_op jit(solution)/shard_map/all_to_all | solution.py:89
  118.4 4.3 %gather_fusion = bf16[1024,128]{1,0:T(8,128)(2,1)} fusion(bf16[4096,128]{1,0:T(8,128)(2,1)S(1)} %bitcast.66, s32[1024]{0:T(1024)S(1)} %broadcast_clamp_fusion), kind=kCustom, calls=%fused_computation | custom fusion | bytes 528384 | tf_op jit(solution)/shard_map/gather | solution.py:96
  (147 shorter events, 22.8 us)
Async XLA Ops:
  0.6 106.0 %copy-start = (bf16[128,128]{1,0:T(8,128)(2,1)S(1)}, bf16[128,128]{1,0:T(8,128)(2,1)}, u32[]{:S(2)}) copy-start(bf16[128,128]{1,0:T(8,128)(2,1)} %param.16) | copy-start | bytes 98308
  0.6 10.2 %copy-start.4 = (s32[1024,1]{0,1:T(1,128)S(1)}, s32[1024,1]{0,1:T(1,128)}, u32[]{:S(2)}) copy-start(s32[1024,1]{0,1:T(1,128)} %param.11) | copy-start | bytes 12292
  16.0 14.4 %all-to-all-start = ((s32[32,1,128]{2,1,0:T(1,128)}), s32[32,1,128]{2,1,0:T(1,128)S(1)}, u32[]{:S(2)}, u32[]{:S(2)}) async-start(s32[32,1,128]{2,1,0:T(1,128)} %bitcast.6), calls=%async_computation | async-start | bytes 32768 | tf_op jit(solution)/shard_map/all_to_all | solution.py:63
  30.5 3.5 %copy-start.2 = (bf16[64,64]{1,0:T(8,128)(2,1)S(1)}, bf16[64,64]{1,0:T(8,128)(2,1)}, u32[]{:S(2)}) copy-start(bf16[64,64]{1,0:T(8,128)(2,1)} %param.15) | copy-start | bytes 24580
  30.5 3.6 %copy-start.3 = (bf16[64,64]{1,0:T(8,128)(2,1)S(1)}, bf16[64,64]{1,0:T(8,128)(2,1)}, u32[]{:S(2)}) copy-start(bf16[64,64]{1,0:T(8,128)(2,1)} %param.14) | copy-start | bytes 24580
  30.5 29.6 %copy-start.5 = (bf16[2048,128]{1,0:T(8,128)(2,1)S(1)}, bf16[2048,128]{1,0:T(8,128)(2,1)}, u32[]{:S(2)}) copy-start(bf16[2048,128]{1,0:T(8,128)(2,1)} %param.13) | copy-start | bytes 1572868
  30.5 29.6 %all-to-all-start.1 = ((bf16[32,128,128]{2,1,0:T(8,128)(2,1)}), bf16[32,128,128]{2,1,0:T(8,128)(2,1)S(1)}, u32[]{:S(2)}, u32[]{:S(2)}) async-start(bf16[32,128,128]{2,1,0:T(8,128)(2,1)} %bitcast.7), calls=%async_computation.1 | async-start | bytes 2097152 | tf_op jit(solution)/shard_map/all_to_all | solution.py:56
  88.6 29.8 %all-to-all-start.2 = ((bf16[32,128,128]{2,1,0:T(8,128)(2,1)}), bf16[32,128,128]{2,1,0:T(8,128)(2,1)S(1)}, u32[]{:S(2)}, u32[]{:S(2)}) async-start(bf16[32,128,128]{2,1,0:T(8,128)(2,1)} %bitcast.11), calls=%async_computation.2 | async-start | bytes 2097152 | tf_op jit(solution)/shard_map/all_to_all | solution.py:89
  92.8 13.7 %copy-start.1 = (bf16[2048,128]{1,0:T(8,128)(2,1)S(1)}, bf16[2048,128]{1,0:T(8,128)(2,1)}, u32[]{:S(2)}) copy-start(bf16[2048,128]{1,0:T(8,128)(2,1)} %param.17) | copy-start | bytes 1572868
  92.9 9.0 %collective-permute-start.2 = (bf16[1,256,128]{2,1,0:T(8,128)(2,1)S(1)}, bf16[1,256,128]{2,1,0:T(8,128)(2,1)S(1)}, u32[]{:S(2)}, u32[]{:S(2)}) collective-permute-start(bf16[1,256,128]{2,1,0:T(8,128)(2,1)S(1)} %get-tuple-element.114), channel_id=1, source_target_pairs={{0,3},{1,2},{2,1},{3,0},{4,7},{5,6},{6,5},{7,4},{8,11},{9,10},{10,... | collective-permute-start | bytes 196616 | tf_op jit(solution)/shard_map/ppermute | solution.py:105
  94.4 11.3 %collective-permute-start.1 = (bf16[1,256,128]{2,1,0:T(8,128)(2,1)S(1)}, bf16[1,256,128]{2,1,0:T(8,128)(2,1)S(1)}, u32[]{:S(2)}, u32[]{:S(2)}) collective-permute-start(bf16[1,256,128]{2,1,0:T(8,128)(2,1)S(1)} %get-tuple-element.115), channel_id=1, source_target_pairs={{0,2},{1,3},{2,0},{3,1},{4,6},{5,7},{6,4},{7,5},{8,10},{9,11},{10,... | collective-permute-start | bytes 196616 | tf_op jit(solution)/shard_map/ppermute | solution.py:105
  94.8 10.9 %collective-permute-start = (bf16[1,256,128]{2,1,0:T(8,128)(2,1)S(1)}, bf16[1,256,128]{2,1,0:T(8,128)(2,1)S(1)}, u32[]{:S(2)}, u32[]{:S(2)}) collective-permute-start(bf16[1,256,128]{2,1,0:T(8,128)(2,1)S(1)} %get-tuple-element.116), channel_id=1, source_target_pairs={{0,1},{1,0},{2,3},{3,2},{4,5},{5,4},{6,7},{7,6},{8,9},{9,8},{10,11... | collective-permute-start | bytes 196616 | tf_op jit(solution)/shard_map/ppermute | solution.py:105
